TPU v7x, 256 devices: a whole 4x4x8 slice. The times are simulated.
256 devices in a mesh: ctx: 32 (over x_lo, z, core), exp: 8 (over y, x_hi).
Axes of the slice: x: 4 (x_hi: 2, x_lo: 2; x = x_hi * 2 + x_lo), y: 4, z: 8, core: 2. Of those that a mesh axis runs over, the one named last changes fastest.
Arguments:
- hidden: bfloat16 [8192, 2048], P(('ctx', 'exp')), may hold values from -1.5 to 1.5
- lengths: int32 [2], replicated, may hold values from 2048 to 4096, as said below
- routes: int32 [8192, 8], P(('ctx', 'exp')), may hold values from 0 to 127, all different within a row; in each aligned block of 32 rows (0 to 31, 32 to 63, ...) at most 4 rows name the same one
- gates: float32 [8192, 8], P(('ctx', 'exp')), may hold values from 0.05 to 0.5
- attn_gain: float32 [2048], replicated, may hold values from 0.25 to 1.75
- q_weight: bfloat16 [2048, 4096], P('ctx', 'exp'), may hold values from -0.125 to 0.125
- key_value_weight: bfloat16 [2048, 1024], P('ctx'), may hold values from -0.125 to 0.125
- q_gain: float32 [128], replicated, may hold values from 0.25 to 1.75
- k_gain: float32 [128], replicated, may hold values from 0.25 to 1.75
- o_weight: bfloat16 [4096, 2048], P('exp', 'ctx'), may hold values from -0.09375 to 0.09375
- moe_gain: float32 [2048], replicated, may hold values from 0.25 to 1.75
- expert_in: bfloat16 [256, 2048, 768], P(('ctx', 'exp')), may hold values from -0.125 to 0.125
- expert_out: bfloat16 [256, 384, 2048], P(('ctx', 'exp')), may hold values from -0.21875 to 0.21875
Outputs:
- new_hidden: bfloat16 [8192, 2048], P(('ctx', 'exp'))
- cache: bfloat16 [2, 8192, 512], P(None, 'ctx', 'exp')
Inputs may be any that keep to these rules, and one draw needn't show every extreme that they name: `lengths`: one of the two prompts has exactly 4096 positions; the other has 2048 to 4096. `routes`: A row names 8 different experts. Within the 32 rows of each device (aligned blocks of rows) no expert is named more than 4 times, a bound that some block reaches.
All inputs are finite; a program needn't handle non-finite values.
Results may differ from a plain program's by a relative error of at most 0.02.
Values may be sent and summed in bfloat16 or wider, within the bound.
No kernel may reach another device: no remote copies, remote signals or barrier semaphores. Data moves between devices by JAX's collectives and lax.ppermute only.
A program may use at most 128 MiB of HBM per device.

v0:
```python
import jax
import jax.numpy as jnp
from jax import lax
from jax.sharding import PartitionSpec as P

MODEL_WIDTH = 2048
QUERY_HEADS = 32
KEY_VALUE_HEADS = 4
HEAD_SIZE = 128
EXPERTS = 128
TOP = 8
epsilon = 1e-06
rope_base = 1000000.0


def from_behind(block, axis, distance):
    devices = range(lax.axis_size(axis))
    route = [((i - distance) % len(devices), i) for i in devices]
    return lax.ppermute(block, axis, route)


def rms_scale(values, gain):
    mean_square = jnp.mean(values * values, axis=-1, keepdims=True)
    return values * lax.rsqrt(mean_square + epsilon) * gain


def mirrored_position(row_ids, count_ctx, tok_ctx):
    half_rows = tok_ctx // 2
    holder = row_ids // tok_ctx
    within = row_ids % tok_ctx
    block_no = jnp.where(within < half_rows, holder, 2 * count_ctx - 1 - holder)
    return block_no * half_rows + within % half_rows


def document_info(token_positions, lengths):
    first_end = lengths[0]
    second_end = lengths[0] + lengths[1]
    document = (token_positions >= first_end).astype(jnp.int32) + (
        token_positions >= second_end
    ).astype(jnp.int32)
    doc_start = jnp.where(document == 0, 0, jnp.where(document == 1, first_end, second_end))
    return (document, token_positions - doc_start)


def rotate(values, rope_pos):
    head_width = values.shape[-1]
    freq_ids = jnp.arange(head_width // 2, dtype=jnp.float32)
    inverse = rope_base ** (-2.0 * freq_ids / head_width)
    angles = rope_pos.astype(jnp.float32)[:, None] * inverse[None, :]
    cosine = jnp.cos(angles)[:, None, :]
    sine_part = jnp.sin(angles)[:, None, :]
    first_half = values[..., : head_width // 2]
    second_half = values[..., head_width // 2 :]
    return jnp.concatenate(
        [
            first_half * cosine - second_half * sine_part,
            second_half * cosine + first_half * sine_part,
        ],
        axis=-1,
    )


def shards(
    hidden,
    lengths,
    routes,
    gates,
    attn_gain,
    q_weight,
    key_value_weight,
    q_gain,
    k_gain,
    o_weight,
    moe_gain,
    expert_in,
    expert_out,
):
    count_ctx = lax.axis_size("ctx")
    expert_count = lax.axis_size("exp")
    my_ctx = lax.axis_index("ctx")
    my_exp = lax.axis_index("exp")
    tok_dev = hidden.shape[0]
    tok_ctx = tok_dev * expert_count
    half_rows = tok_ctx // 2
    head_groups = QUERY_HEADS // KEY_VALUE_HEADS
    q_dev = QUERY_HEADS // expert_count
    key_value_share = max(1, KEY_VALUE_HEADS // expert_count)
    group_dev = q_dev // key_value_share
    column_share = KEY_VALUE_HEADS * HEAD_SIZE // expert_count
    key_value_leading = my_exp * q_dev // head_groups
    col_offset = my_exp * column_share - key_value_leading * HEAD_SIZE
    score_scale = HEAD_SIZE ** (-0.5)
    query_pos = mirrored_position(
        my_ctx * tok_ctx + jnp.arange(tok_ctx, dtype=jnp.int32), count_ctx, tok_ctx
    )
    query_doc, query_rope = document_info(query_pos, lengths)
    normed_own = rms_scale(hidden.astype(jnp.float32), attn_gain).astype(jnp.bfloat16)
    normed = lax.all_gather(normed_own, "exp", axis=0, tiled=True)
    key_cols = lax.dynamic_slice_in_dim(
        key_value_weight, key_value_leading * HEAD_SIZE, key_value_share * HEAD_SIZE, 1
    )
    value_column_block = lax.dynamic_slice_in_dim(
        key_value_weight,
        KEY_VALUE_HEADS * HEAD_SIZE + key_value_leading * HEAD_SIZE,
        key_value_share * HEAD_SIZE,
        1,
    )
    kv_local = jnp.concatenate([key_cols, value_column_block], axis=1)
    q_width = q_dev * HEAD_SIZE
    weights_all = lax.all_gather(
        jnp.concatenate([q_weight, kv_local], axis=1), "ctx", axis=0, tiled=True
    )
    projected = jnp.dot(normed, weights_all, preferred_element_type=jnp.float32)
    q_raw = projected[:, :q_width]
    key_value_plain = projected[:, q_width:]
    queries = rotate(
        rms_scale(q_raw.reshape(tok_ctx, q_dev, HEAD_SIZE), q_gain), query_rope
    ).astype(jnp.bfloat16)
    key_row_block = rotate(
        rms_scale(
            key_value_plain[:, : key_value_share * HEAD_SIZE].reshape(
                tok_ctx, key_value_share, HEAD_SIZE
            ),
            k_gain,
        ),
        query_rope,
    ).astype(jnp.bfloat16)
    value_row_block = key_value_plain[:, key_value_share * HEAD_SIZE :].astype(jnp.bfloat16)
    key_values = jnp.stack(
        [key_row_block.reshape(tok_ctx, key_value_share * HEAD_SIZE), value_row_block]
    )
    query_groups = queries.reshape(tok_ctx, key_value_share, group_dev, HEAD_SIZE)

    def attend(state_now, block_kv, offset):
        length_now = block_kv.shape[1]
        key_pos = mirrored_position(
            offset + jnp.arange(length_now, dtype=jnp.int32), count_ctx, tok_ctx
        )
        key_doc, unused_rope = document_info(key_pos, lengths)
        allowed = (query_doc[:, None] == key_doc[None, :]) & (
            key_pos[None, :] <= query_pos[:, None]
        )
        key_part = block_kv[0].reshape(length_now, key_value_share, HEAD_SIZE)
        value_part = block_kv[1].reshape(length_now, key_value_share, HEAD_SIZE)
        scores = (
            jnp.einsum("qkgd,skd->kgqs", query_groups, key_part, preferred_element_type=jnp.float32)
            * score_scale
        )
        weights = jnp.where(allowed[None, None], jnp.exp(scores), 0.0).astype(jnp.bfloat16)
        numerator = state_now[0] + jnp.einsum(
            "kgqs,skd->qkgd", weights, value_part, preferred_element_type=jnp.float32
        )
        denominator = state_now[1] + jnp.sum(weights, axis=-1, dtype=jnp.float32)
        return (numerator, denominator) + tuple(state_now[2:])

    initial = (
        jnp.zeros((tok_ctx, key_value_share, group_dev, HEAD_SIZE), jnp.float32),
        jnp.zeros((key_value_share, group_dev, tok_ctx), jnp.float32),
    )
    every_kv = lax.all_gather(key_values, "ctx", axis=1, tiled=True)
    total_rows = every_kv.shape[1]
    chunk = min(1024, total_rows)

    def turn(step_no, state_now):
        block_kv = lax.dynamic_slice_in_dim(every_kv, step_no * chunk, chunk, 1)
        return attend(state_now, block_kv, step_no * chunk)

    final_state = lax.fori_loop(0, total_rows // chunk, turn, initial)
    context = (
        (final_state[0] / jnp.transpose(final_state[1], (2, 0, 1))[..., None])
        .astype(jnp.bfloat16)
        .reshape(tok_ctx, q_dev * HEAD_SIZE)
    )

    def block_start(block_no):
        holder = jnp.where(block_no < count_ctx, block_no, 2 * count_ctx - 1 - block_no)
        return holder * tok_ctx + jnp.where(block_no < count_ctx, 0, half_rows)

    first_part = lax.dynamic_slice(
        every_kv, (0, block_start(2 * my_ctx), col_offset), (2, half_rows, column_share)
    )
    second_part = lax.dynamic_slice(
        every_kv, (0, block_start(2 * my_ctx + 1), col_offset), (2, half_rows, column_share)
    )
    cache = jnp.concatenate([first_part, second_part], axis=1)
    attn_part = jnp.dot(
        context,
        lax.all_gather(o_weight, "ctx", axis=1, tiled=True),
        preferred_element_type=jnp.float32,
    )
    attn_own = lax.psum_scatter(
        attn_part.astype(jnp.bfloat16), "exp", scatter_dimension=0, tiled=True
    ).astype(jnp.float32)
    residual_mid = hidden.astype(jnp.float32) + attn_own
    moe_in = rms_scale(residual_mid, moe_gain).astype(jnp.bfloat16)
    devices = count_ctx * expert_count
    slices = max(1, devices // EXPERTS)
    rows_dev = expert_in.shape[0]
    ffs_dev = expert_out.shape[1]
    capacity = max(4, 2 * tok_dev * TOP // EXPERTS)
    route_ids = routes.reshape(-1)
    route_count = route_ids.shape[0]
    expert_hot = (route_ids[:, None] == jnp.arange(EXPERTS, dtype=jnp.int32)[None, :]).astype(
        jnp.int32
    )
    ranking = jnp.sum(jnp.cumsum(expert_hot, axis=0) * expert_hot, axis=1) - 1
    slot_ids = route_ids * capacity + ranking
    slot_hot = (
        slot_ids[:, None] == jnp.arange(EXPERTS * capacity, dtype=jnp.int32)[None, :]
    ).astype(jnp.bfloat16)
    token_hot = (
        (jnp.arange(route_count, dtype=jnp.int32) // TOP)[:, None]
        == jnp.arange(tok_dev, dtype=jnp.int32)[None, :]
    ).astype(jnp.bfloat16)
    placement_map = jnp.einsum(
        "rs,rt->st", slot_hot, token_hot, preferred_element_type=jnp.float32
    ).astype(jnp.bfloat16)
    outgoing = jnp.dot(placement_map, moe_in, preferred_element_type=jnp.float32).astype(
        jnp.bfloat16
    )
    experts_ctx = EXPERTS // count_ctx
    outgoing = outgoing.reshape(count_ctx, experts_ctx * capacity, MODEL_WIDTH)
    landed = lax.all_to_all(outgoing, "ctx", split_axis=0, concat_axis=0, tiled=True)
    landed = jnp.broadcast_to(
        landed.reshape(count_ctx, experts_ctx, 1, capacity, MODEL_WIDTH),
        (count_ctx, experts_ctx, slices, capacity, MODEL_WIDTH),
    ).reshape(count_ctx, expert_count, capacity, MODEL_WIDTH)
    arrived = lax.all_to_all(landed, "exp", split_axis=1, concat_axis=1, tiled=True)
    arrived = arrived.reshape(count_ctx, expert_count, rows_dev, capacity, MODEL_WIDTH)
    gate_up = jnp.einsum("abrcd,rdf->abrcf", arrived, expert_in, preferred_element_type=jnp.float32)
    activated = (jax.nn.silu(gate_up[..., :ffs_dev]) * gate_up[..., ffs_dev:]).astype(jnp.bfloat16)
    produced = jnp.einsum(
        "abrcf,rfd->abrcd", activated, expert_out, preferred_element_type=jnp.float32
    ).astype(jnp.bfloat16)
    produced = produced.reshape(count_ctx, expert_count, rows_dev * capacity, MODEL_WIDTH)
    came_back = lax.all_to_all(produced, "exp", split_axis=1, concat_axis=1, tiled=True)
    part_sum = jnp.sum(
        came_back.reshape(count_ctx, experts_ctx, slices, capacity, MODEL_WIDTH),
        axis=2,
        dtype=jnp.float32,
    ).astype(jnp.bfloat16)
    returned = lax.all_to_all(
        part_sum.reshape(count_ctx, experts_ctx * capacity, MODEL_WIDTH),
        "ctx",
        split_axis=0,
        concat_axis=0,
        tiled=True,
    )
    slice_sum = returned.reshape(EXPERTS * capacity, MODEL_WIDTH).astype(jnp.float32)
    gate_hot = slot_hot.astype(jnp.float32) * gates.reshape(-1)[:, None]
    combiner = jnp.einsum(
        "rs,rt->ts", gate_hot, token_hot.astype(jnp.float32), precision=lax.Precision.HIGHEST
    )
    moe_out = jnp.dot(combiner, slice_sum, precision=lax.Precision.HIGHEST)
    new_hidden = (residual_mid + moe_out).astype(jnp.bfloat16)
    return (new_hidden, cache)


def solution(mesh):
    in_specs = (
        P(("ctx", "exp"), None),
        P(),
        P(("ctx", "exp"), None),
        P(("ctx", "exp"), None),
        P(),
        P("ctx", "exp"),
        P("ctx", None),
        P(),
        P(),
        P("exp", "ctx"),
        P(),
        P(("ctx", "exp"), None, None),
        P(("ctx", "exp"), None, None),
    )
    out_specs = (P(("ctx", "exp"), None), P(None, "ctx", "exp"))
    return jax.shard_map(shards, mesh=mesh, in_specs=in_specs, out_specs=out_specs, check_vma=False)
```

profile of v0, /device:TPU:32, one launch (start us, length us, event | category | flops | bytes accessed | tf_op | source)
XLA Modules:
  0.0 614.3 jit_solution(10730122127005586213)
XLA Ops:
  7.2 1.2 fusion.46
  8.4 1.7 fusion.48
  10.9 1.5 pad_maximum_fusion.3
  12.5 1.3 fusion.84
  15.8 49.4 %all-gather.5.cloned.1.call-done = bf16[256,2048]{1,0:T(8,128)(2,1)} async-done(((bf16[32,2048]{1,0:T(8,128)(2,1)}), bf16[256,2048]{1,0:T(8,128)(2,1)}) %all-gather.5.cloned.1.call-update) | async-done | bytes 1048592 | tf_op jit(solution)/shard_map/all_gather | solution.py:98
  65.2 65.6 %all-gather.7.cloned.1.call-done = bf16[2048,768]{1,0:T(8,128)(2,1)} async-done(((bf16[64,768]{1,0:T(8,128)(2,1)}), bf16[2048,768]{1,0:T(8,128)(2,1)}) %all-gather.7.cloned.1.call-update) | async-done | bytes 3145744 | tf_op jit(solution)/shard_map/all_gather | solution.py:110
  130.8 3.2 fusion.85
  136.9 2.3 fusion.83
  139.1 2.0 reshape.532
  141.1 1.4 multiply_reduce_fusion
  142.6 1.2 fusion.41
  144.3 57.5 %all-gather.9.cloned.1.call-done = bf16[2,8192,128]{2,1,0:T(8,128)(2,1)} async-done(((bf16[2,256,128]{2,1,0:T(8,128)(2,1)}), bf16[2,8192,128]{2,1,0:T(8,128)(2,1)}) %all-gather.9.cloned.1.call-update) | async-done | bytes 4194320 | tf_op jit(solution)/shard_map/all_gather | solution.py:160
  201.9 44.5 %while.21 = (s32[]{:T(128)}, f32[256,1,4,128]{0,3,2,1:T(8,128)}, f32[1,4,256]{2,1,0:T(4,128)S(1)}, bf16[2,8192,128]{2,1,0:T(8,128)(2,1)}, s32[2]{0:T(128)S(1)}, ...) while((s32[]{:T(128)}, f32[256,1,4,128]{0,3,2,1:T(8,128)}, ...), condition=%wide.region_5.6_spmd.clone.clone.clone, body=%wide.region_3.5_spmd.clone.clone.clone.sunk | while | flops 543215872 | bytes 10785070 | solution.py:168
  202.9 2.1 convert_reduce_fusion.2
  205.1 1.5 fusion.99
  208.5 2.1 convert_reduce_fusion.2
  210.6 1.5 fusion.99
  214.0 2.1 convert_reduce_fusion.2
  216.2 1.5 fusion.99
  219.6 2.1 convert_reduce_fusion.2
  221.8 1.5 fusion.99
  225.2 2.1 convert_reduce_fusion.2
  227.3 1.5 fusion.99
  230.7 2.1 convert_reduce_fusion.2
  232.9 1.5 fusion.99
  236.3 2.1 convert_reduce_fusion.2
  238.4 1.5 fusion.99
  241.8 2.1 convert_reduce_fusion.2
  244.0 1.5 fusion.99
  247.5 20.4 %all-gather.11.cloned.1.call-done = bf16[512,2048]{0,1:T(8,128)(2,1)} async-done(((bf16[512,64]{0,1:T(8,128)(2,1)}), bf16[512,2048]{0,1:T(8,128)(2,1)}) %all-gather.11.cloned.1.call-update) | async-done | bytes 2097168 | tf_op jit(solution)/shard_map/all_gather | solution.py:188
  267.9 3.3 convolution_convert_fusion.2
  272.1 77.6 %reduce-scatter.2.cloned.1.call-done = bf16[32,2048]{1,0:T(8,128)(2,1)} async-done(((bf16[256,2048]{1,0:T(8,128)(2,1)}), bf16[32,2048]{1,0:T(8,128)(2,1)}) %reduce-scatter.2.cloned.1.call-update) | async-done | bytes 131088 | tf_op jit(solution)/shard_map/reduce_scatter | solution.py:191
  350.8 3.2 convolution_convert_fusion.1
  354.0 59.3 %all_to_all.20 = bf16[32,16,2048]{2,1,0:T(8,128)(2,1)} all-to-all(bf16[32,16,2048]{2,1,0:T(8,128)(2,1)} %bitcast.128), channel_id=1, replica_groups=mesh['ctx'=32,'exp'=8] {'ctx'}, dimensions={0} | all-to-all | bytes 4194304 | tf_op jit(solution)/shard_map/all_to_all | solution.py:223
  413.4 4.2 broadcast_in_dim.90
  417.5 2.6 copy.100
  420.1 2.6 broadcast_in_dim.91
  422.7 54.6 %all_to_all.21 = bf16[32,8,4,2048]{3,2,0,1:T(4,128)(2,1)S(1)} all-to-all(bf16[32,8,4,2048]{3,2,0,1:T(4,128)(2,1)S(1)} %bitcast.127), channel_id=1, replica_groups=mesh['ctx'=32,'exp'=8] {'exp'}, dimensions={1} | all-to-all | bytes 8388608 | tf_op jit(solution)/shard_map/all_to_all | solution.py:228
  477.3 5.0 fusion.32
  482.3 2.4 convolution_convert_fusion
  484.7 3.2 copy.102
  487.9 51.5 %all_to_all.22 = bf16[32,8,4,2048]{3,2,0,1:T(4,128)(2,1)S(1)} all-to-all(bf16[32,8,4,2048]{3,2,0,1:T(4,128)(2,1)S(1)} %copy.102), channel_id=1, replica_groups=mesh['ctx'=32,'exp'=8] {'exp'}, dimensions={1} | all-to-all | bytes 8388608 | tf_op jit(solution)/shard_map/all_to_all | solution.py:236
  539.4 3.4 bitcast_reduce_fusion
  542.8 1.2 copy.104
  543.9 2.5 copy.105
  546.4 6.4 %all-to-all-start.3 = ((bf16[32,16,2048]{2,1,0:T(8,128)(2,1)}), bf16[32,16,2048]{2,1,0:T(8,128)(2,1)}, u32[]{:S(2)}, u32[]{:S(2)}) async-start(bf16[32,16,2048]{2,1,0:T(8,128)(2,1)} %copy.105), calls=%async_computation.4 | async-start | bytes 4194304 | tf_op jit(solution)/shard_map/all_to_all | solution.py:242
  555.9 48.5 %all-to-all-done.3 = bf16[32,16,2048]{2,1,0:T(8,128)(2,1)} async-done(((bf16[32,16,2048]{2,1,0:T(8,128)(2,1)}), bf16[32,16,2048]{2,1,0:T(8,128)(2,1)}, u32[]{:S(2)}, u32[]{:S(2)}) %all-to-all-start.3) | async-done | bytes 2097184 | tf_op jit(solution)/shard_map/all_to_all | solution.py:242
  604.4 3.4 fusion.31
  (135 shorter events, 25.6 us)
Async XLA Ops:
  7.2 470.2 %copy-start = (bf16[1,2048,768]{2,1,0:T(8,128)(2,1)S(1)}, bf16[1,2048,768]{2,1,0:T(8,128)(2,1)}, u32[]{:S(2)}) copy-start(bf16[1,2048,768]{2,1,0:T(8,128)(2,1)} %param.26) | copy-start | bytes 9437188
  7.2 58.0 %all-gather.5.cloned.1.call-start = ((), (), s32[]{:S(2)}) async-start(), calls=%async_computation.5 | async-start | bytes 1179648 | tf_op jit(solution)/shard_map/all_gather | solution.py:98
  10.1 120.7 %all-gather.7.cloned.1.call-start = ((), (), s32[]{:S(2)}) async-start(), calls=%async_computation.6 | async-start | bytes 3244032 | tf_op jit(solution)/shard_map/all_gather | solution.py:110
  10.2 124.0 %copy-start.10 = (f32[128]{0:T(128)S(1)}, f32[128]{0:T(128)}, u32[]{:S(2)}) copy-start(f32[128]{0:T(128)} %param.23) | copy-start | bytes 1540
  12.5 189.4 %all-gather.9.cloned.1.call-start = ((), (), s32[]{:S(2)}) async-start(), calls=%async_computation.7 | async-start | bytes 4325376 | tf_op jit(solution)/shard_map/all_gather | solution.py:160
  134.0 0.9 copy-start.5
  134.0 8.6 %copy-start.11 = (f32[128]{0:T(128)S(1)}, f32[128]{0:T(128)}, u32[]{:S(2)}) copy-start(f32[128]{0:T(128)} %param.22) | copy-start | bytes 1540
  135.7 132.2 %all-gather.11.cloned.1.call-start = ((), (), s32[]{:S(2)}) async-start(), calls=%async_computation.8 | async-start | bytes 2162688 | tf_op jit(solution)/shard_map/all_gather | solution.py:188
  136.3 213.5 %reduce-scatter.2.cloned.1.call-start = ((), (), s32[]{:S(2)}) async-start(), calls=%async_computation.9 | async-start | bytes 1179648 | tf_op jit(solution)/shard_map/reduce_scatter | solution.py:191
  139.1 62.7 %copy-start.6 = (s32[2]{0:T(128)S(1)}, s32[2]{0:T(128)}, u32[]{:S(2)}) copy-start(s32[2]{0:T(128)} %param.16) | copy-start | bytes 28
  202.9 2.2 copy-start.1
  206.6 0.8 copy-start.2
  208.5 2.2 copy-start.1
  212.2 0.8 copy-start.2
  214.0 2.2 copy-start.1
  217.7 0.8 copy-start.2
  219.6 2.2 copy-start.1
  223.3 0.8 copy-start.2
  225.2 2.2 copy-start.1
  228.8 0.8 copy-start.2
  230.7 2.2 copy-start.1
  234.4 0.8 copy-start.2
  236.3 2.2 copy-start.1
  240.0 0.8 copy-start.2
  241.8 2.2 copy-start.1
  245.5 0.8 copy-start.2
  246.3 24.9 %copy-start.8 = (s32[32,8]{0,1:T(8,128)S(1)}, s32[32,8]{0,1:T(8,128)}, u32[]{:S(2)}) copy-start(s32[32,8]{0,1:T(8,128)} %param.17) | copy-start | bytes 3076
  246.3 103.4 %copy-start.3 = (bf16[32,2048]{1,0:T(8,128)(2,1)S(1)}, bf16[32,2048]{1,0:T(8,128)(2,1)}, u32[]{:S(2)}) copy-start(bf16[32,2048]{1,0:T(8,128)(2,1)} %param.15) | copy-start | bytes 393220
  246.3 104.5 %copy-start.7 = (f32[2048]{0:T(1024)S(1)}, f32[2048]{0:T(1024)}, u32[]{:S(2)}) copy-start(f32[2048]{0:T(1024)} %param.25) | copy-start | bytes 24580
  477.3 5.0 copy-start.12
  546.4 6.5 %copy-start.9 = (f32[32,8]{0,1:T(8,128)S(1)}, f32[32,8]{0,1:T(8,128)}, u32[]{:S(2)}) copy-start(f32[32,8]{0,1:T(8,128)} %param.18) | copy-start | bytes 3076
  546.4 57.9 %copy-start.4 = (bf16[32,2048]{1,0:T(8,128)(2,1)S(1)}, bf16[32,2048]{1,0:T(8,128)(2,1)}, u32[]{:S(2)}) copy-start(bf16[32,2048]{1,0:T(8,128)(2,1)} %reduce-scatter.2.cloned.1.call-done) | copy-start | bytes 393220
  546.4 57.9 %all-to-all-start.3 = ((bf16[32,16,2048]{2,1,0:T(8,128)(2,1)}), bf16[32,16,2048]{2,1,0:T(8,128)(2,1)}, u32[]{:S(2)}, u32[]{:S(2)}) async-start(bf16[32,16,2048]{2,1,0:T(8,128)(2,1)} %copy.105), calls=%async_computation.4 | async-start | bytes 4194304 | tf_op jit(solution)/shard_map/all_to_all | solution.py:242
Sparse Core Ops, SparseCore 0:
  11.2 53.9 all-gather.4
  67.1 63.6 all-gather.6
  135.8 66.0 all-gather.8
  203.6 64.2 all-gather.10
  271.6 78.0 reduce-scatter.1
where the time goes:
time: 616 us; the launch traced here: 614 us
  waiting for transfers between devices  320 us (52%)
  blocking collectives  165 us (27%)
  matrix products  50.8 us (8%)
  local copies, waits for them, and re-layouts  31.3 us (5%)
  other arithmetic  24.7 us (4%)
  between operations  15.4 us (2%)
  starting transfers between devices  6.63 us (1%)
    reduce_scatter x1, waiting for transfers between devices, shards(): lax.psum_scatter(attn_part.astype(jnp.bfloat16), 'exp', scatter_dimension...  77.6 us
    all_gather x1, waiting for transfers between devices, shards(): lax.all_gather(jnp.concatenate([q_weight, kv_local], axis=1), 'ctx', axis...  65.6 us
    all_to_all x1, blocking collectives, shards(): lax.all_to_all(outgoing, 'ctx', split_axis=0, concat_axis=0, tiled=True)  59.3 us
    all_gather x1, waiting for transfers between devices, shards(): every_kv = lax.all_gather(key_values, 'ctx', axis=1, tiled=True)  57.5 us
    all_to_all x1, blocking collectives, shards(): lax.all_to_all(landed, 'exp', split_axis=1, concat_axis=1, tiled=True)  54.6 us
    all_to_all x1, blocking collectives, shards(): lax.all_to_all(produced, 'exp', split_axis=1, concat_axis=1, tiled=True)  51.5 us
    all_gather x1, waiting for transfers between devices, shards(): normed = lax.all_gather(normed_own, 'exp', axis=0, tiled=True)  49.4 us
    all_to_all x1, waiting for transfers between devices, shards(): lax.all_to_all(part_sum.reshape(count_ctx, experts_ctx * capacity, MODEL_...  48.5 us
  transfers between devices with their start and end apart: 6, of which 6 were waited for; matrix products, arithmetic and copies ran while one was open for 9% of the time, Pallas kernels for 0%

commit v1 on v0

--- a/solution.py
+++ b/solution.py
@@ -157,7 +157,9 @@
         jnp.zeros((tok_ctx, key_value_share, group_dev, HEAD_SIZE), jnp.float32),
         jnp.zeros((key_value_share, group_dev, tok_ctx), jnp.float32),
     )
-    every_kv = lax.all_gather(key_values, "ctx", axis=1, tiled=True)
+    every_kv = jnp.concatenate(
+        lax.all_to_all(jnp.stack([key_values for _ in range(lax.psum(1, "ctx"))]), "ctx", 0, 0), 1
+    )
     total_rows = every_kv.shape[1]
     chunk = min(1024, total_rows)
 

time: 616 us -> 648 us (1.052)
  waiting for transfers between devices: 320 us -> 336 us
  local copies, waits for them, and re-layouts: 31.3 us -> 40 us
  starting transfers between devices: 6.63 us -> 14.2 us
    all_to_all x0 -> x1, waiting for transfers between devices: none -> 97.7 us  [shards(): lax.all_to_all(jnp.stack([key_values for _ in range(lax.psum(1, 'ctx'))])...]
    all_gather x1 -> x0, waiting for transfers between devices: 57.5 us -> none  [shards(): every_kv = lax.all_gather(key_values, 'ctx', axis=1, tiled=True)]
    all_gather x1, waiting for transfers between devices: 20.4 us -> 0.02 us  [shards(): lax.all_gather(o_weight, 'ctx', axis=1, tiled=True)]
    all_to_all x0 -> x1, starting transfers between devices: none -> 7.57 us  [shards(): lax.all_to_all(jnp.stack([key_values for _ in range(lax.psum(1, 'ctx'))])...]
  transfers between devices with their start and end apart: 6 -> 6, of which waited for: 6 -> 5; matrix products, arithmetic and copies ran while one was open for 9% -> 9% of each run, Pallas kernels for 0% -> 0%
where the time goes in v1:
time: 648 us; the launch traced here: 647 us
  waiting for transfers between devices  336 us (52%)
  blocking collectives  165 us (25%)
  matrix products  50.8 us (8%)
  local copies, waits for them, and re-layouts  40 us (6%)
  other arithmetic  24.3 us (4%)
  between operations  15.5 us (2%)
  starting transfers between devices  14.2 us (2%)
    all_to_all x1, waiting for transfers between devices, shards(): lax.all_to_all(jnp.stack([key_values for _ in range(lax.psum(1, 'ctx'))])...  97.7 us
    reduce_scatter x1, waiting for transfers between devices, shards(): lax.psum_scatter(attn_part.astype(jnp.bfloat16), 'exp', scatter_dimension...  74.3 us
    all_gather x1, waiting for transfers between devices, shards(): lax.all_gather(jnp.concatenate([q_weight, kv_local], axis=1), 'ctx', axis...  65.6 us
    all_to_all x1, blocking collectives, shards(): lax.all_to_all(outgoing, 'ctx', split_axis=0, concat_axis=0, tiled=True)  59.3 us
    all_to_all x1, blocking collectives, shards(): lax.all_to_all(landed, 'exp', split_axis=1, concat_axis=1, tiled=True)  54.5 us
    all_to_all x1, blocking collectives, shards(): lax.all_to_all(produced, 'exp', split_axis=1, concat_axis=1, tiled=True)  51.5 us
    all_gather x1, waiting for transfers between devices, shards(): normed = lax.all_gather(normed_own, 'exp', axis=0, tiled=True)  49.4 us
    all_to_all x1, waiting for transfers between devices, shards(): lax.all_to_all(part_sum.reshape(count_ctx, experts_ctx * capacity, MODEL_...  48.5 us
  transfers between devices with their start and end apart: 6, of which 5 were waited for; matrix products, arithmetic and copies ran while one was open for 9% of the time, Pallas kernels for 0%

profile of v1, /device:TPU:32, one launch (start us, length us, event | category | flops | bytes accessed | tf_op | source)
XLA Modules:
  0.0 646.8 jit_solution(16787845431506172240)
XLA Ops:
  8.4 1.7 fusion.48
  11.0 1.5 pad_maximum_fusion.3
  12.5 1.3 fusion.84
  15.8 49.4 %all-gather.4.cloned.1.call-done = bf16[256,2048]{1,0:T(8,128)(2,1)} async-done(((bf16[32,2048]{1,0:T(8,128)(2,1)}), bf16[256,2048]{1,0:T(8,128)(2,1)}) %all-gather.4.cloned.1.call-update) | async-done | bytes 1048592 | tf_op jit(solution)/shard_map/all_gather | solution.py:98
  65.2 65.6 %all-gather.6.cloned.1.call-done = bf16[2048,768]{1,0:T(8,128)(2,1)} async-done(((bf16[64,768]{1,0:T(8,128)(2,1)}), bf16[2048,768]{1,0:T(8,128)(2,1)}) %all-gather.6.cloned.1.call-update) | async-done | bytes 3145744 | tf_op jit(solution)/shard_map/all_gather | solution.py:110
  130.8 3.2 fusion.85
  135.1 2.5 stack.8
  137.6 7.6 %all-to-all-start = ((bf16[32,2,256,128]{2,3,1,0:T(8,128)(2,1)}), bf16[32,2,256,128]{2,3,1,0:T(8,128)(2,1)}, u32[]{:S(2)}, u32[]{:S(2)}) async-start(bf16[32,2,256,128]{2,3,1,0:T(8,128)(2,1)} %stack.8), calls=%async_computation | async-start | bytes 8388608 | tf_op jit(solution)/shard_map/all_to_all | solution.py:161
  146.5 2.2 fusion.83
  148.7 2.0 reshape.542
  150.7 1.4 multiply_reduce_fusion
  152.2 1.2 fusion.41
  153.9 97.7 %all-to-all-done = bf16[32,2,256,128]{2,3,1,0:T(8,128)(2,1)} async-done(((bf16[32,2,256,128]{2,3,1,0:T(8,128)(2,1)}), bf16[32,2,256,128]{2,3,1,0:T(8,128)(2,1)}, u32[]{:S(2)}, u32[]{:S(2)}) %all-to-all-start) | async-done | bytes 4194336 | tf_op jit(solution)/shard_map/all_to_all | solution.py:161
  251.6 6.4 copy.103
  257.9 44.6 %while.21 = (s32[]{:T(128)}, f32[256,1,4,128]{0,3,2,1:T(8,128)}, f32[1,4,256]{2,1,0:T(4,128)S(1)}, bf16[2,8192,128]{2,1,0:T(8,128)(2,1)}, s32[2]{0:T(128)S(1)}, ...) while((s32[]{:T(128)}, f32[256,1,4,128]{0,3,2,1:T(8,128)}, ...), condition=%wide.region_5.6_spmd.clone.clone.clone, body=%wide.region_3.5_spmd.clone.clone.clone.sunk | while | flops 543215872 | bytes 10785070 | solution.py:170
  259.0 2.1 convert_reduce_fusion.2
  261.2 1.5 fusion.99
  264.6 2.1 convert_reduce_fusion.2
  266.8 1.5 fusion.99
  270.2 2.1 convert_reduce_fusion.2
  272.3 1.5 fusion.99
  275.8 2.1 convert_reduce_fusion.2
  277.9 1.5 fusion.99
  281.3 2.1 convert_reduce_fusion.2
  283.5 1.5 fusion.99
  286.9 2.1 convert_reduce_fusion.2
  289.1 1.5 fusion.99
  292.5 2.1 convert_reduce_fusion.2
  294.6 1.5 fusion.99
  298.1 2.1 convert_reduce_fusion.2
  300.2 1.5 fusion.99
  303.7 3.3 convolution_convert_fusion.2
  307.9 74.3 %reduce-scatter.2.cloned.1.call-done = bf16[32,2048]{1,0:T(8,128)(2,1)} async-done(((bf16[256,2048]{1,0:T(8,128)(2,1)}), bf16[32,2048]{1,0:T(8,128)(2,1)}) %reduce-scatter.2.cloned.1.call-update) | async-done | bytes 131088 | tf_op jit(solution)/shard_map/reduce_scatter | solution.py:193
  383.3 3.2 convolution_convert_fusion.1
  386.5 59.3 %all_to_all.25 = bf16[32,16,2048]{2,1,0:T(8,128)(2,1)} all-to-all(bf16[32,16,2048]{2,1,0:T(8,128)(2,1)} %bitcast.131), channel_id=1, replica_groups=mesh['ctx'=32,'exp'=8] {'ctx'}, dimensions={0} | all-to-all | bytes 4194304 | tf_op jit(solution)/shard_map/all_to_all | solution.py:225
  445.9 4.2 broadcast_in_dim.90
  450.0 2.6 copy.111
  452.6 2.6 broadcast_in_dim.91
  455.2 54.5 %all_to_all.26 = bf16[32,8,4,2048]{3,2,0,1:T(4,128)(2,1)S(1)} all-to-all(bf16[32,8,4,2048]{3,2,0,1:T(4,128)(2,1)S(1)} %bitcast.130), channel_id=1, replica_groups=mesh['ctx'=32,'exp'=8] {'exp'}, dimensions={1} | all-to-all | bytes 8388608 | tf_op jit(solution)/shard_map/all_to_all | solution.py:230
  509.8 5.0 fusion.32
  514.8 2.3 convolution_convert_fusion
  517.1 3.2 copy.113
  520.4 51.5 %all_to_all.27 = bf16[32,8,4,2048]{3,2,0,1:T(4,128)(2,1)S(1)} all-to-all(bf16[32,8,4,2048]{3,2,0,1:T(4,128)(2,1)S(1)} %copy.113), channel_id=1, replica_groups=mesh['ctx'=32,'exp'=8] {'exp'}, dimensions={1} | all-to-all | bytes 8388608 | tf_op jit(solution)/shard_map/all_to_all | solution.py:238
  571.9 3.4 bitcast_reduce_fusion
  576.4 2.5 copy.116
  578.9 6.4 all-to-all-start.4
  588.3 48.5 %all-to-all-done.4 = bf16[32,16,2048]{2,1,0:T(8,128)(2,1)} async-done(((bf16[32,16,2048]{2,1,0:T(8,128)(2,1)}), bf16[32,16,2048]{2,1,0:T(8,128)(2,1)}, u32[]{:S(2)}, u32[]{:S(2)}) %all-to-all-start.4) | async-done | bytes 2097184 | tf_op jit(solution)/shard_map/all_to_all | solution.py:244
  636.8 3.4 fusion.31
  (139 shorter events, 27.8 us)
Async XLA Ops:
  7.2 502.6 %copy-start = (bf16[1,2048,768]{2,1,0:T(8,128)(2,1)S(1)}, bf16[1,2048,768]{2,1,0:T(8,128)(2,1)}, u32[]{:S(2)}) copy-start(bf16[1,2048,768]{2,1,0:T(8,128)(2,1)} %param.26) | copy-start | bytes 9437188
  7.2 58.0 %all-gather.4.cloned.1.call-start = ((), (), s32[]{:S(2)}) async-start(), calls=%async_computation.6 | async-start | bytes 1179648 | tf_op jit(solution)/shard_map/all_gather | solution.py:98
  10.1 120.7 %all-gather.6.cloned.1.call-start = ((), (), s32[]{:S(2)}) async-start(), calls=%async_computation.7 | async-start | bytes 3244032 | tf_op jit(solution)/shard_map/all_gather | solution.py:110
  10.2 124.0 %copy-start.11 = (f32[128]{0:T(128)S(1)}, f32[128]{0:T(128)}, u32[]{:S(2)}) copy-start(f32[128]{0:T(128)} %param.23) | copy-start | bytes 1540
  134.0 0.9 copy-start.6
  137.6 114.0 %all-to-all-start = ((bf16[32,2,256,128]{2,3,1,0:T(8,128)(2,1)}), bf16[32,2,256,128]{2,3,1,0:T(8,128)(2,1)}, u32[]{:S(2)}, u32[]{:S(2)}) async-start(bf16[32,2,256,128]{2,3,1,0:T(8,128)(2,1)} %stack.8), calls=%async_computation | async-start | bytes 8388608 | tf_op jit(solution)/shard_map/all_to_all | solution.py:161
  145.1 7.0 %copy-start.12 = (f32[128]{0:T(128)S(1)}, f32[128]{0:T(128)}, u32[]{:S(2)}) copy-start(f32[128]{0:T(128)} %param.22) | copy-start | bytes 1540
  145.2 158.5 %all-gather.8.cloned.1.call-start = ((), (), s32[]{:S(2)}) async-start(), calls=%async_computation.8 | async-start | bytes 2162688 | tf_op jit(solution)/shard_map/all_gather | solution.py:190
  145.9 236.3 %reduce-scatter.2.cloned.1.call-start = ((), (), s32[]{:S(2)}) async-start(), calls=%async_computation.9 | async-start | bytes 1179648 | tf_op jit(solution)/shard_map/reduce_scatter | solution.py:193
  153.9 104.1 %copy-start.7 = (s32[2]{0:T(128)S(1)}, s32[2]{0:T(128)}, u32[]{:S(2)}) copy-start(s32[2]{0:T(128)} %param.16) | copy-start | bytes 28
  259.0 2.2 copy-start.2
  262.7 0.8 copy-start.3
  264.6 2.2 copy-start.2
  268.3 0.8 copy-start.3
  270.2 2.2 copy-start.2
  273.9 0.8 copy-start.3
  275.8 2.1 copy-start.2
  279.4 0.8 copy-start.3
  281.3 2.2 copy-start.2
  285.0 0.8 copy-start.3
  286.9 2.2 copy-start.2
  290.6 0.8 copy-start.3
  292.5 2.1 copy-start.2
  296.2 0.8 copy-start.3
  298.1 2.2 copy-start.2
  301.8 0.8 copy-start.3
  302.6 4.5 copy-start.9
  302.6 79.7 %copy-start.4 = (bf16[32,2048]{1,0:T(8,128)(2,1)S(1)}, bf16[32,2048]{1,0:T(8,128)(2,1)}, u32[]{:S(2)}) copy-start(bf16[32,2048]{1,0:T(8,128)(2,1)} %param.15) | copy-start | bytes 393220
  302.6 80.7 %copy-start.8 = (f32[2048]{0:T(1024)S(1)}, f32[2048]{0:T(1024)}, u32[]{:S(2)}) copy-start(f32[2048]{0:T(1024)} %param.25) | copy-start | bytes 24580
  509.8 5.0 copy-start.13
  576.4 63.8 %copy-start.1 = (bf16[1,2048,768]{2,1,0:T(8,128)(2,1)S(1)}, bf16[1,2048,768]{2,1,0:T(8,128)(2,1)}, u32[]{:S(2)}) copy-start(bf16[1,2048,768]{2,1,0:T(8,128)(2,1)} %param.26) | copy-start | bytes 9437188
  578.9 6.5 %copy-start.10 = (f32[32,8]{0,1:T(8,128)S(1)}, f32[32,8]{0,1:T(8,128)}, u32[]{:S(2)}) copy-start(f32[32,8]{0,1:T(8,128)} %param.18) | copy-start | bytes 3076
  578.9 57.9 %copy-start.5 = (bf16[32,2048]{1,0:T(8,128)(2,1)S(1)}, bf16[32,2048]{1,0:T(8,128)(2,1)}, u32[]{:S(2)}) copy-start(bf16[32,2048]{1,0:T(8,128)(2,1)} %reduce-scatter.2.cloned.1.call-done) | copy-start | bytes 393220
  578.9 57.9 %all-to-all-start.4 = ((bf16[32,16,2048]{2,1,0:T(8,128)(2,1)}), bf16[32,16,2048]{2,1,0:T(8,128)(2,1)}, u32[]{:S(2)}, u32[]{:S(2)}) async-start(bf16[32,16,2048]{2,1,0:T(8,128)(2,1)} %copy.116), calls=%async_computation.5 | async-start | bytes 4194304 | tf_op jit(solution)/shard_map/all_to_all | solution.py:244
Sparse Core Ops, SparseCore 0:
  11.2 53.9 all-gather.3
  67.1 63.6 all-gather.5
  147.8 80.3 all-gather.7
  307.2 74.9 reduce-scatter.1
